TPU v7x, 32 devices: a whole 2x2x4 slice. The times are simulated.
32 devices in a mesh: day: 4 (over z), dom: 8 (over y, x, core).
Axes of the slice: x: 2, y: 2, z: 4, core: 2. Of those that a mesh axis runs over, the one named last changes fastest.
Arguments:
- node_states: bfloat16 [16, 2048, 256], P('day', 'dom'), may hold values from -12 to 12
- edge_source: int32 [16, 8192], P('day', 'dom'), may hold values from 0 to 383
- edge_target: int32 [16, 8192], P('day', 'dom'), may hold values from 0 to 255
- halo_rows: int32 [16, 1024], P('day', 'dom'), may hold values from 0 to 255
- halo_count: int32 [16, 8], P('day', 'dom'), may hold values from 1 to 128, 640 in all within a row
- w_message: bfloat16 [256, 256], replicated, may hold values from -0.375 to 0.375
- w_query: bfloat16 [256, 256], replicated, may hold values from -1 to 1, as said below
- w_key: bfloat16 [256, 256], replicated, may hold values from -1 to 1, as said below
- w_value: bfloat16 [256, 256], replicated, may hold values from -0.375 to 0.375
- cotangent: bfloat16 [16, 8, 4, 64, 256], P(None, 'dom', 'day'), may hold values from -6 to 6
Outputs:
- state_grad: float32 [16, 2048, 256], P('day', 'dom')
- grad_message: float32 [256, 256], replicated
- grad_query: float32 [256, 256], replicated
- grad_key: float32 [256, 256], replicated
- grad_value: float32 [256, 256], replicated
Inputs may be any that keep to these rules, and one draw needn't show every extreme that they name: `edge_source`: indices of the extended rows: below 256 a partition's own account, from 256 on a received halo slot. `halo_rows`: rows of the sending partition's own block; repeats allowed. `halo_count`: on every day some partition has all 128 slots live. `w_query`: entries of order 256 ** -0.5. `w_key`: entries of order 256 ** -0.5.
All inputs are finite; a program needn't handle non-finite values. No bound on the sum of `halo_count` on one device may be relied on, other than what follows from the above.
Results may differ from a plain program's by a relative error of at most 0.004.
The roundings to bfloat16 on the way count: a program that leaves them out, or rounds other values in their place, can miss the bound.
Values may be sent and summed in bfloat16 or wider, within the bound.
No kernel may reach another device: no remote copies, remote signals or barrier semaphores. Data moves between devices by JAX's collectives and lax.ppermute only.
A program may use at most 64 MiB of HBM per device.

v0:
```python
import jax
import jax.numpy as jnp
from jax import lax
from jax.sharding import PartitionSpec as P

HEADS = 4


def from_behind(value, axis, steps):
    count = lax.axis_size(axis)
    pairs = [(source, (source + steps) % count) for source in range(count)]
    return lax.ppermute(value, axis, pairs)


def adjacency(sources, targets, count_rows, total_rows):
    target_hot = (targets[:, None] == jnp.arange(count_rows, dtype=jnp.int32)[None, :]).astype(
        jnp.bfloat16
    )
    source_hot = (sources[:, None] == jnp.arange(total_rows, dtype=jnp.int32)[None, :]).astype(
        jnp.bfloat16
    )
    counts = lax.dot_general(
        target_hot, source_hot, (((0,), (0,)), ((), ())), preferred_element_type=jnp.float32
    )
    return counts.astype(jnp.bfloat16)


def gnn_forward(states, received, adjacent, w_message):
    extended = jnp.concatenate([states, received], axis=0)
    neighbours = jnp.dot(adjacent, extended, preferred_element_type=jnp.float32)
    counted = jnp.sum(adjacent.astype(jnp.float32), axis=1)
    inverse = 1.0 / (counted + 1.0)
    aggregate = ((states.astype(jnp.float32) + neighbours) * inverse[:, None]).astype(jnp.bfloat16)
    preact = jnp.dot(aggregate, w_message, preferred_element_type=jnp.float32)
    hidden = (states.astype(jnp.float32) + jax.nn.silu(preact)).astype(jnp.bfloat16)
    return (aggregate, preact, inverse, hidden)


def gnn_backward(upstream, aggregate, preact, inverse, adjacent, w_message):
    count_rows = aggregate.shape[0]
    up_float = upstream.astype(jnp.float32)
    sigmoid_val = jax.nn.sigmoid(preact)
    pre_grad = (up_float * sigmoid_val * (1.0 + preact * (1.0 - sigmoid_val))).astype(jnp.bfloat16)
    message_part = lax.dot_general(
        aggregate, pre_grad, (((0,), (0,)), ((), ())), preferred_element_type=jnp.float32
    )
    agg_grad = lax.dot_general(
        pre_grad, w_message, (((1,), (1,)), ((), ())), preferred_element_type=jnp.float32
    )
    term_grad = agg_grad * inverse[:, None]
    ext_grad = lax.dot_general(
        adjacent.astype(jnp.float32),
        term_grad,
        (((0,), (0,)), ((), ())),
        precision=lax.Precision.HIGHEST,
        preferred_element_type=jnp.float32,
    )
    local_grad = up_float + term_grad + ext_grad[:count_rows]
    halo_grad = ext_grad[count_rows:].astype(jnp.bfloat16)
    return (message_part, local_grad, halo_grad)


def attend(states, upstream, w_query, w_key, w_value):
    steps_all, nodes_here, width = states.shape
    head_dim = width // HEADS
    scale_factor = head_dim ** (-0.5)
    flat = states.reshape(steps_all * nodes_here, width)

    def project(weight):
        return jnp.dot(flat, weight, preferred_element_type=jnp.float32).astype(jnp.bfloat16)

    def splitter(matrix):
        return matrix.reshape(steps_all, nodes_here, HEADS, head_dim).astype(jnp.float32)

    queries = project(w_query)
    key_rows = project(w_key)
    value_rows = project(w_value)
    query_f = splitter(queries)
    key_f = splitter(key_rows)
    value_f = splitter(value_rows)
    scores = jnp.einsum("tnhd,snhd->nhts", query_f, key_f) * scale_factor
    causal = jnp.arange(steps_all)[:, None] >= jnp.arange(steps_all)[None, :]
    scores = jnp.where(causal, scores, -jnp.inf)
    highest = jnp.max(scores, axis=-1, keepdims=True)
    exponent = jnp.exp(scores - highest)
    probs = exponent / jnp.sum(exponent, axis=-1, keepdims=True)
    probs_low = probs.astype(jnp.bfloat16).astype(jnp.float32)
    up_heads = splitter(upstream)
    value_grad = jnp.einsum("nhts,tnhd->snhd", probs_low, up_heads).astype(jnp.bfloat16)
    prob_grad = jnp.einsum("tnhd,snhd->nhts", up_heads, value_f)
    score_grad = (
        probs * (prob_grad - jnp.sum(prob_grad * probs, axis=-1, keepdims=True)) * scale_factor
    ).astype(jnp.bfloat16)
    score_f = score_grad.astype(jnp.float32)
    query_grad = jnp.einsum("nhts,snhd->tnhd", score_f, key_f).astype(jnp.bfloat16)
    key_grad = jnp.einsum("nhts,tnhd->snhd", score_f, query_f).astype(jnp.bfloat16)
    query_flat = query_grad.reshape(steps_all * nodes_here, width)
    key_flat = key_grad.reshape(steps_all * nodes_here, width)
    value_flat = value_grad.reshape(steps_all * nodes_here, width)

    def weight_grad(grad_rows):
        return lax.dot_general(
            flat, grad_rows, (((0,), (0,)), ((), ())), preferred_element_type=jnp.float32
        )

    def input_grad(grad_rows, weight):
        return lax.dot_general(
            grad_rows, weight, (((1,), (1,)), ((), ())), preferred_element_type=jnp.float32
        )

    back = upstream.reshape(steps_all * nodes_here, width).astype(jnp.float32)
    back = (
        back
        + input_grad(query_flat, w_query)
        + input_grad(key_flat, w_key)
        + input_grad(value_flat, w_value)
    )
    back = back.astype(jnp.bfloat16).reshape(steps_all, nodes_here, width)
    return ((weight_grad(query_flat), weight_grad(key_flat), weight_grad(value_flat)), back)


def local(
    node_states,
    edge_source,
    edge_target,
    halo_rows,
    halo_count,
    w_message,
    w_query,
    w_key,
    w_value,
    cotangent,
):
    days_local, node_local, width = node_states.shape
    halo_slots = halo_rows.shape[1]
    live = jnp.arange(halo_slots)[None, :] < halo_count
    picked = jnp.take_along_axis(node_states, halo_rows[:, :, None], axis=1)
    sent = jnp.where(live[:, :, None], picked, jnp.zeros_like(picked))
    received = from_behind(sent, "dom", 1)

    def forward_one(items):
        adjacent = adjacency(items[2], items[3], node_local, node_local + halo_slots)
        aggregate, preact, inverse, hidden = gnn_forward(items[0], items[1], adjacent, w_message)
        return (aggregate, preact, inverse, hidden, adjacent)

    aggregate, preact, inverse, hidden, adjacent = lax.map(
        forward_one, (node_states, received, edge_source, edge_target)
    )
    node_major = lax.all_to_all(hidden, "day", split_axis=1, concat_axis=0, tiled=True)
    upstream = cotangent.reshape(cotangent.shape[0], -1, width)
    attn_grads, back = attend(node_major, upstream, w_query, w_key, w_value)
    back_days = lax.all_to_all(back, "day", split_axis=0, concat_axis=1, tiled=True)

    def backward_one(items):
        return gnn_backward(items[0], items[1], items[2], items[3], items[4], w_message)

    message_parts, local_grad, halo_grad = lax.map(
        backward_one, (back_days, aggregate, preact, inverse, adjacent)
    )
    grad_message = jnp.sum(message_parts, axis=0)
    returned = from_behind(halo_grad, "dom", -1)
    slot_hot = jnp.logical_and(
        halo_rows[:, :, None] == jnp.arange(node_local, dtype=jnp.int32)[None, None, :],
        live[:, :, None],
    ).astype(jnp.bfloat16)
    scattered = jnp.einsum("dsn,dsh->dnh", slot_hot, returned, preferred_element_type=jnp.float32)
    state_grad = local_grad + scattered
    grad_message, grad_query, grad_key, grad_value = lax.psum(
        (grad_message, attn_grads[0], attn_grads[1], attn_grads[2]), ("day", "dom")
    )
    return (state_grad, grad_message, grad_query, grad_key, grad_value)


def solution(mesh):
    return jax.shard_map(
        local,
        mesh=mesh,
        in_specs=(
            P("day", "dom", None),
            P("day", "dom"),
            P("day", "dom"),
            P("day", "dom"),
            P("day", "dom"),
            P(),
            P(),
            P(),
            P(),
            P(None, "dom", "day", None, None),
        ),
        out_specs=(P("day", "dom", None), P(), P(), P(), P()),
        check_vma=False,
    )
```

profile of v0, /device:TPU:0, one launch (start us, length us, event | category | flops | bytes accessed | tf_op | source)
XLA Modules:
  0.0 277.3 jit_solution(9602864403409959612)
XLA Ops:
  7.2 0.7 fusion.70
  7.9 0.8 iota_compare_fusion.8
  8.7 7.0 %gather_fusion = bf16[512,256]{1,0:T(8,128)(2,1)S(1)} fusion(bf16[4,256,256]{2,1,0:T(8,128)(2,1)} %param.14, s32[512]{0:T(512)S(1)} %fusion.70), kind=kCustom, calls=%fused_computation | custom fusion | bytes 528384 | tf_op jit(solution)/shard_map/jit(take_along_axis)/gather | solution.py:137
  16.4 6.9 %collective-permute-done = bf16[4,128,256]{2,1,0:T(8,128)(2,1)S(1)} collective-permute-done((bf16[4,128,256]{2,1,0:T(8,128)(2,1)S(1)}, bf16[4,128,256]{2,1,0:T(8,128)(2,1)S(1)}, u32[]{:S(2)}, u32[]{:S(2)}) %collective-permute-start) | collective-permute-done | bytes 262176 | tf_op jit(solution)/shard_map/ppermute | solution.py:12
  23.4 12.2 %while.34 = (s32[]{:T(128)}, bf16[4,256,256]{2,1,0:T(8,128)(2,1)S(1)}, f32[4,256,256]{2,1,0:T(8,128)S(1)}, f32[4,256]{1,0:T(4,128)S(1)}, bf16[4,256,256]{2,1,0:T...) while((s32[]{:T(128)}, ...), condition=%wide.region_2.3_spmd.clone, body=%wide.region_0.2_spmd.sunk.clone | while | flops 287277312 | bytes 3111561 | solution.py:146
  23.5 0.7 constant_dynamic-slice_fusion.7
  24.2 1.0 convert_reduce_fusion.3
  25.8 0.7 bitcast_dynamic-update-slice_fusion.15
  26.5 0.7 constant_dynamic-slice_fusion.7
  27.3 1.0 convert_reduce_fusion.3
  28.8 0.7 bitcast_dynamic-update-slice_fusion.15
  29.5 0.7 constant_dynamic-slice_fusion.7
  30.3 1.0 convert_reduce_fusion.3
  31.8 0.7 bitcast_dynamic-update-slice_fusion.15
  32.6 0.7 constant_dynamic-slice_fusion.7
  33.3 1.0 convert_reduce_fusion.3
  34.9 0.7 bitcast_dynamic-update-slice_fusion.15
  35.6 1.2 copy.52
  36.9 5.6 %all-to-all-start = ((bf16[4,256,256]{2,0,1:T(4,128)(2,1)}), bf16[4,256,256]{2,0,1:T(4,128)(2,1)S(1)}, u32[]{:S(2)}, u32[]{:S(2)}) async-start(bf16[4,256,256]{2,0,1:T(4,128)(2,1)} %copy.52), calls=%async_computation | async-start | bytes 1048576 | tf_op jit(solution)/shard_map/all_to_all | solution.py:149
  42.9 12.5 %all-to-all-done = bf16[4,256,256]{2,0,1:T(4,128)(2,1)S(1)} async-done(((bf16[4,256,256]{2,0,1:T(4,128)(2,1)}), bf16[4,256,256]{2,0,1:T(4,128)(2,1)S(1)}, u32[]{:S(2)}, u32[]{:S(2)}) %all-to-all-start) | async-done | bytes 524320 | tf_op jit(solution)/shard_map/all_to_all | solution.py:149
  55.8 1.4 reshape.100
  57.5 1.4 reshape.99
  59.6 2.6 fusion.52
  62.3 4.9 %fusion.77 = (f32[64,4,16]{2,1,0:T(4,128)S(1)}, f32[64,4,16,16]{2,3,1,0:T(8,128)}) fusion(pred[16,16]{0,1:T(8,128)(4,1)S(1)} %iota_compare_fusion.7, bf16[16,64,4,64]{3,2,1,0:T(4,128)(2,1)} %reshape.99, bf16[16,64,4,64]{3,2,1,0:T(4,128)(2,1)} %reshape.100), kind=kOutput, calls=%fused_computation.119 | convolution fusion | flops 8650767 | bytes 1327360 | tf_op jit(solution)/shard_map/sub | solution.py:85
  67.2 5.8 %fusion.50 = bf16[16,64,4,64]{3,0,2,1:T(8,128)(2,1)} fusion(f32[64,4,16,16]{3,2,1,0:T(8,128)} %fusion.52, bf16[16,64,4,64]{3,2,1,0:T(4,128)(2,1)S(1)} %copy-done.5, f32[64,4,16,16]{2,3,1,0:T(8,128)} %get-tuple-element.183, f32[64,4,16]{2,1,0:T(4,128)S(1)} %get-tuple-element.182), kind=kOutput, calls=%fused_computation.78 | convolution fusion | flops 9113615 | bytes 1589248 | tf_op jit(solution)/shard_map/nhts,tnhd->snhd/dot_general | solution.py:96
  73.0 6.1 %fusion.48 = bf16[16,64,4,64]{3,0,2,1:T(8,128)(2,1)} fusion(f32[64,4,16,16]{3,2,1,0:T(8,128)} %fusion.52, bf16[16,64,4,64]{3,2,1,0:T(4,128)(2,1)} %reshape.99, f32[64,4,16,16]{2,3,1,0:T(8,128)} %get-tuple-element.183, f32[64,4,16]{2,1,0:T(4,128)S(1)} %get-tuple-element.182), kind=kOutput, calls=%fused_computation.76 | convolution fusion | flops 9113615 | bytes 1589248 | tf_op jit(solution)/shard_map/nhts,snhd->tnhd/dot_general | solution.py:95
  79.2 3.5 %fusion.49 = bf16[16,64,4,64]{3,0,2,1:T(8,128)(2,1)} fusion(bf16[16,64,4,64]{3,2,1,0:T(4,128)(2,1)S(1)} %reshape_reshape.4, f32[64,4,16,16]{2,3,1,0:T(8,128)} %get-tuple-element.183, f32[64,4,16]{2,1,0:T(4,128)} %copy-done.13), kind=kOutput, calls=%fused_computation.77 | convolution fusion | flops 8781824 | bytes 1327104 | tf_op jit(solution)/shard_map/nhts,tnhd->snhd/dot_general | solution.py:89
  82.7 1.7 copy.63
  84.4 0.7 reshape.103
  85.2 3.1 %copy.61 = bf16[16,64,4,64]{1,0,3,2:T(8,128)(2,1)S(1)} copy(bf16[16,64,4,64]{3,0,2,1:T(8,128)(2,1)} %fusion.48) | data formatting | bytes 1048576 | tf_op jit(solution)/shard_map/convert_element_type | solution.py:95
  88.3 0.7 reshape.102
  89.0 2.9 %copy.65 = bf16[16,64,4,64]{1,0,3,2:T(8,128)(2,1)S(1)} copy(bf16[16,64,4,64]{3,0,2,1:T(8,128)(2,1)} %fusion.49) | data formatting | bytes 1048576 | tf_op jit(solution)/shard_map/convert_element_type | solution.py:89
  91.9 0.7 reshape.104
  92.7 1.4 convolution_add_fusion.3
  94.5 1.2 fusion.51
  95.6 3.5 %all-to-all-start.1 = ((bf16[16,64,256]{2,1,0:T(8,128)(2,1)}), bf16[16,64,256]{2,1,0:T(8,128)(2,1)S(1)}, u32[]{:S(2)}, u32[]{:S(2)}) async-start(bf16[16,64,256]{2,1,0:T(8,128)(2,1)} %bitcast.30), calls=%async_computation.1 | async-start | bytes 1048576 | tf_op jit(solution)/shard_map/all_to_all | solution.py:152
  99.2 1.0 fusion.87
  100.2 1.0 fusion.86
  101.3 10.9 %all-to-all-done.1 = bf16[16,64,256]{2,1,0:T(8,128)(2,1)S(1)} async-done(((bf16[16,64,256]{2,1,0:T(8,128)(2,1)}), bf16[16,64,256]{2,1,0:T(8,128)(2,1)S(1)}, u32[]{:S(2)}, u32[]{:S(2)}) %all-to-all-start.1) | async-done | bytes 524320 | tf_op jit(solution)/shard_map/all_to_all | solution.py:152
  112.1 0.8 copy.66
  113.1 18.6 %while.35 = (s32[]{:T(128)}, f32[4,256,256]{2,1,0:T(8,128)S(1)}, f32[4,256,256]{2,1,0:T(8,128)S(1)}, bf16[4,128,256]{2,1,0:T(8,128)(2,1)}, bf16[4,256,256]{2,1,0...) while((s32[]{:T(128)}, f32[4,256,256]{2,1,0:T(8,128)S(1)}, ...), condition=%wide.region_7.8_spmd.clone, body=%wide.region_6.7_spmd.sunk.clone | while | flops 370671616 | bytes 5576841 | solution.py:157
  113.2 1.3 convolution_multiply_fusion.3
  114.5 1.3 fusion.149
  115.8 0.6 fusion.151
  116.5 1.3 fusion.148
  117.8 1.3 convolution_multiply_fusion.3
  119.1 1.3 fusion.149
  120.5 0.6 fusion.151
  121.1 1.3 fusion.148
  122.5 1.3 convolution_multiply_fusion.3
  123.8 1.3 fusion.149
  125.8 1.3 fusion.148
  127.1 1.3 convolution_multiply_fusion.3
  128.4 1.3 fusion.149
  130.4 1.3 fusion.148
  131.8 1.1 fusion.88
  132.9 0.8 reduce_sum.38
  133.7 2.3 collective-permute-done.1
  136.0 2.4 convolution_add_fusion.4
  138.5 125.3 %all-reduce.3.cloned.1.call-done = (f32[256,256]{1,0:T(8,128)}, f32[256,256]{1,0:T(8,128)}, f32[256,256]{1,0:T(8,128)}, f32[256,256]{1,0:T(8,128)}) async-done(((f32[256,256]{1,0:T(8,128)}, f32[256,256]{1,0:T(8,128)}, f32[256,256]{1,0:T(8,128)}, f32[256,256]{1,0:T(8,128)}), (f32[256,256]{1,0:T(8,128)}, f32[256,256]{1,0:T(8,128)}, f32[256,256]{1,0:T(8,128)}, ...) | async-done | bytes 1048592 | tf_op jit(solution)/shard_map/psum | solution.py:168
  263.8 1.7 copy.137
  265.5 1.7 copy.138
  267.1 1.7 copy.139
  268.8 1.7 copy.140
  (94 shorter events, 7.1 us)
Async XLA Ops:
  7.2 48.3 %copy-start = (bf16[256,256]{1,0:T(8,128)(2,1)S(1)}, bf16[256,256]{1,0:T(8,128)(2,1)}, u32[]{:S(2)}) copy-start(bf16[256,256]{1,0:T(8,128)(2,1)} %param.20) | copy-start | bytes 393220
  8.7 14.8 %copy-start.1 = (bf16[4,256,256]{2,1,0:T(8,128)(2,1)S(1)}, bf16[4,256,256]{2,1,0:T(8,128)(2,1)}, u32[]{:S(2)}) copy-start(bf16[4,256,256]{2,1,0:T(8,128)(2,1)} %param.14) | copy-start | bytes 1572868
  8.7 14.8 %copy-start.2 = (bf16[256,256]{1,0:T(8,128)(2,1)S(1)}, bf16[256,256]{1,0:T(8,128)(2,1)}, u32[]{:S(2)}) copy-start(bf16[256,256]{1,0:T(8,128)(2,1)} %param.19) | copy-start | bytes 393220
  15.9 7.4 %collective-permute-start = (bf16[4,128,256]{2,1,0:T(8,128)(2,1)S(1)}, bf16[4,128,256]{2,1,0:T(8,128)(2,1)S(1)}, u32[]{:S(2)}, u32[]{:S(2)}) collective-permute-start(bf16[4,128,256]{2,1,0:T(8,128)(2,1)S(1)} %select_select_fusion), channel_id=1, source_target_pairs={{0,1},{1,2},{2,3},{3,4},{4,5},{5,6},{6,7},{7,0},{8,9},{9,10},{10,1... | collective-permute-start | bytes 786440 | tf_op jit(solution)/shard_map/ppermute | solution.py:12
  35.6 1.2 copy-start.6
  35.6 19.8 %copy-start.12 = (bf16[4,256,256]{2,1,0:T(8,128)(2,1)}, bf16[4,256,256]{2,1,0:T(8,128)(2,1)S(1)}, u32[]{:S(2)}) copy-start(bf16[4,256,256]{2,1,0:T(8,128)(2,1)S(1)} %get-tuple-element.422) | copy-start | bytes 1572868
  35.6 6.8 %copy-start.4 = (bf16[16,1,1,64,256]{4,3,2,1,0:T(8,128)(2,1)S(1)}, bf16[16,1,1,64,256]{4,3,2,1,0:T(8,128)(2,1)}, u32[]{:S(2)}) copy-start(bf16[16,1,1,64,256]{4,3,2,1,0:T(8,128)(2,1)} %param.23) | copy-start | bytes 1572868
  36.9 18.5 %all-to-all-start = ((bf16[4,256,256]{2,0,1:T(4,128)(2,1)}), bf16[4,256,256]{2,0,1:T(4,128)(2,1)S(1)}, u32[]{:S(2)}, u32[]{:S(2)}) async-start(bf16[4,256,256]{2,0,1:T(4,128)(2,1)} %copy.52), calls=%async_computation | async-start | bytes 1048576 | tf_op jit(solution)/shard_map/all_to_all | solution.py:149
  55.4 1.8 copy-start.9
  55.8 3.1 %copy-start.8 = (bf16[256,256]{1,0:T(8,128)(2,1)S(1)}, bf16[256,256]{1,0:T(8,128)(2,1)}, u32[]{:S(2)}) copy-start(bf16[256,256]{1,0:T(8,128)(2,1)} %param.22) | copy-start | bytes 393220
  62.3 5.0 %copy-start.5 = (bf16[16,64,4,64]{3,2,1,0:T(4,128)(2,1)S(1)}, bf16[16,64,4,64]{3,2,1,0:T(4,128)(2,1)}, u32[]{:S(2)}) copy-start(bf16[16,64,4,64]{3,2,1,0:T(4,128)(2,1)} %reshape.100) | copy-start | bytes 1572868
  67.2 5.8 %copy-start.13 = (f32[64,4,16]{2,1,0:T(4,128)}, f32[64,4,16]{2,1,0:T(4,128)S(1)}, u32[]{:S(2)}) copy-start(f32[64,4,16]{2,1,0:T(4,128)S(1)} %get-tuple-element.182) | copy-start | bytes 49156
  79.2 3.5 %copy-start.7 = (bf16[16,64,4,64]{3,0,2,1:T(8,128)(2,1)S(1)}, bf16[16,64,4,64]{3,0,2,1:T(8,128)(2,1)}, u32[]{:S(2)}) copy-start(bf16[16,64,4,64]{3,0,2,1:T(8,128)(2,1)} %fusion.50) | copy-start | bytes 1572868
  92.7 1.5 copy-start.10
  95.6 16.5 %all-to-all-start.1 = ((bf16[16,64,256]{2,1,0:T(8,128)(2,1)}), bf16[16,64,256]{2,1,0:T(8,128)(2,1)S(1)}, u32[]{:S(2)}, u32[]{:S(2)}) async-start(bf16[16,64,256]{2,1,0:T(8,128)(2,1)} %bitcast.30), calls=%async_computation.1 | async-start | bytes 1048576 | tf_op jit(solution)/shard_map/all_to_all | solution.py:152
  99.1 164.7 %all-reduce.3.cloned.1.call-start = ((), (), s32[]{:S(2)}) async-start(), calls=%async_computation.2 | async-start | bytes 2097152 | tf_op jit(solution)/shard_map/psum | solution.py:168
  113.2 2.6 copy-start.3
  117.8 2.6 copy-start.3
  122.5 2.6 copy-start.3
  127.1 2.6 copy-start.3
  131.8 4.3 %copy-start.11 = (s32[4,128]{1,0:T(4,128)S(1)}, s32[4,128]{1,0:T(4,128)}, u32[]{:S(2)}) copy-start(s32[4,128]{1,0:T(4,128)} %param.17) | copy-start | bytes 6148
  131.8 4.3 %collective-permute-start.1 = (bf16[4,128,256]{2,1,0:T(8,128)(2,1)}, bf16[4,128,256]{2,1,0:T(8,128)(2,1)}, u32[]{:S(2)}, u32[]{:S(2)}) collective-permute-start(bf16[4,128,256]{2,1,0:T(8,128)(2,1)} %get-tuple-element.126), channel_id=1, source_target_pairs={{0,7},{1,0},{2,1},{3,2},{4,3},{5,4},{6,5},{7,6},{8,15},{9,8},{10,9... | collective-permute-start | bytes 786440 | tf_op jit(solution)/shard_map/ppermute | solution.py:12
Sparse Core Ops, SparseCore 0:
  133.8 129.9 all-reduce.2
where the time goes:
time: 278 us; the launch traced here: 277 us
  waiting for transfers between devices  158 us (57%)
  matrix products  53.5 us (19%)
  local copies, waits for them, and re-layouts  38.3 us (14%)
  between operations  14.4 us (5%)
  starting transfers between devices  9.7 us (3%)
  other arithmetic  3.06 us (1%)
    psum x1, waiting for transfers between devices, local(): lax.psum((grad_message, attn_grads[0], attn_grads[1], attn_grads[2]), ('d...  125 us
    all_to_all x1, waiting for transfers between devices, local(): lax.all_to_all(hidden, 'day', split_axis=1, concat_axis=0, tiled=True)  12.5 us
    all_to_all x1, waiting for transfers between devices, local(): lax.all_to_all(back, 'day', split_axis=0, concat_axis=1, tiled=True)  10.9 us
    ppermute x2, waiting for transfers between devices, from_behind(): return lax.ppermute(value, axis, pairs)  9.28 us
    gather x1, local copies, waits for them, and re-layouts, local(): picked = jnp.take_along_axis(node_states, halo_rows[:, :, None], axis=1)  7 us
    unnamed x30, local copies, waits for them, and re-layouts  6.74 us
    dot_general x1, matrix products, attend(): jnp.einsum('nhts,snhd->tnhd', score_f, key_f).astype(jnp.bfloat16)  6.14 us
    dot_general x1, matrix products, attend(): jnp.einsum('nhts,tnhd->snhd', score_f, query_f).astype(jnp.bfloat16)  5.79 us
  transfers between devices with their start and end apart: 5, of which 5 were waited for; matrix products, arithmetic and copies ran while one was open for 2% of the time, Pallas kernels for 0%

commit v1 on v0

--- a/solution.py
+++ b/solution.py
@@ -166,7 +166,7 @@
     scattered = jnp.einsum("dsn,dsh->dnh", slot_hot, returned, preferred_element_type=jnp.float32)
     state_grad = local_grad + scattered
     grad_message, grad_query, grad_key, grad_value = lax.psum(
-        (grad_message, attn_grads[0], attn_grads[1], attn_grads[2]), ("day", "dom")
+        lax.psum((grad_message, attn_grads[0], attn_grads[1], attn_grads[2]), "dom"), "day"
     )
     return (state_grad, grad_message, grad_query, grad_key, grad_value)
 

time: 278 us -> 254 us (0.914)
  waiting for transfers between devices: 158 us -> 138 us
  local copies, waits for them, and re-layouts: 38.3 us -> 35 us
    psum x1 -> x2, waiting for transfers between devices: 125 us -> 105 us  [the longest x1 56 us: local(): lax.psum((grad_message, attn_grads[0], attn_grads[1], attn_grads[2]), 'dom')]
  transfers between devices with their start and end apart: 5 -> 6, of which waited for: 5 -> 6; matrix products, arithmetic and copies ran while one was open for 2% -> 2% of each run, Pallas kernels for 0% -> 0%
where the time goes in v1:
time: 254 us; the launch traced here: 253 us
  waiting for transfers between devices  138 us (54%)
  matrix products  52.2 us (21%)
  local copies, waits for them, and re-layouts  35 us (14%)
  between operations  14.4 us (6%)
  starting transfers between devices  9.74 us (4%)
  other arithmetic  3.08 us (1%)
    psum x1, waiting for transfers between devices, local(): lax.psum((grad_message, attn_grads[0], attn_grads[1], attn_grads[2]), 'dom')  56 us
    psum x1, waiting for transfers between devices, local(): lax.psum(lax.psum((grad_message, attn_grads[0], attn_grads[1], attn_grads...  49.2 us
    all_to_all x1, waiting for transfers between devices, local(): lax.all_to_all(hidden, 'day', split_axis=1, concat_axis=0, tiled=True)  12.5 us
    ppermute x2, waiting for transfers between devices, from_behind(): return lax.ppermute(value, axis, pairs)  10.8 us
    all_to_all x1, waiting for transfers between devices, local(): lax.all_to_all(back, 'day', split_axis=0, concat_axis=1, tiled=True)  9.83 us
    gather x1, local copies, waits for them, and re-layouts, local(): picked = jnp.take_along_axis(node_states, halo_rows[:, :, None], axis=1)  7 us
    unnamed x30, local copies, waits for them, and re-layouts  6.74 us
    dot_general x1, matrix products, attend(): jnp.einsum('nhts,snhd->tnhd', score_f, key_f).astype(jnp.bfloat16)  6.16 us
  transfers between devices with their start and end apart: 6, of which 6 were waited for; matrix products, arithmetic and copies ran while one was open for 2% of the time, Pallas kernels for 0%

profile of v1, /device:TPU:0, one launch (start us, length us, event | category | flops | bytes accessed | tf_op | source)
XLA Modules:
  0.0 253.2 jit_solution(2209630299610362486)
XLA Ops:
  7.2 0.7 fusion.70
  7.9 0.8 iota_compare_fusion.8
  8.7 7.0 %gather_fusion = bf16[512,256]{1,0:T(8,128)(2,1)S(1)} fusion(bf16[4,256,256]{2,1,0:T(8,128)(2,1)} %param.14, s32[512]{0:T(512)S(1)} %fusion.70), kind=kCustom, calls=%fused_computation | custom fusion | bytes 528384 | tf_op jit(solution)/shard_map/jit(take_along_axis)/gather | solution.py:137
  15.9 0.5 collective-permute-start
  16.4 6.9 %collective-permute-done = bf16[4,128,256]{2,1,0:T(8,128)(2,1)S(1)} collective-permute-done((bf16[4,128,256]{2,1,0:T(8,128)(2,1)S(1)}, bf16[4,128,256]{2,1,0:T(8,128)(2,1)S(1)}, u32[]{:S(2)}, u32[]{:S(2)}) %collective-permute-start) | collective-permute-done | bytes 262176 | tf_op jit(solution)/shard_map/ppermute | solution.py:12
  23.4 12.2 %while.34 = (s32[]{:T(128)}, bf16[4,256,256]{2,1,0:T(8,128)(2,1)S(1)}, f32[4,256,256]{2,1,0:T(8,128)S(1)}, f32[4,256]{1,0:T(4,128)S(1)}, bf16[4,256,256]{2,1,0:T...) while((s32[]{:T(128)}, ...), condition=%wide.region_2.3_spmd.clone, body=%wide.region_0.2_spmd.sunk.clone | while | flops 287277312 | bytes 3111561 | solution.py:146
  23.5 0.7 constant_dynamic-slice_fusion.7
  24.2 1.0 convert_reduce_fusion.3
  25.8 0.7 bitcast_dynamic-update-slice_fusion.15
  26.5 0.7 constant_dynamic-slice_fusion.7
  27.2 1.0 convert_reduce_fusion.3
  28.8 0.7 bitcast_dynamic-update-slice_fusion.15
  29.5 0.7 constant_dynamic-slice_fusion.7
  30.3 1.0 convert_reduce_fusion.3
  31.8 0.7 bitcast_dynamic-update-slice_fusion.15
  32.6 0.7 constant_dynamic-slice_fusion.7
  33.3 1.0 convert_reduce_fusion.3
  34.9 0.7 bitcast_dynamic-update-slice_fusion.15
  35.6 1.2 copy.52
  36.8 5.6 %all-to-all-start = ((bf16[4,256,256]{2,0,1:T(4,128)(2,1)}), bf16[4,256,256]{2,0,1:T(4,128)(2,1)S(1)}, u32[]{:S(2)}, u32[]{:S(2)}) async-start(bf16[4,256,256]{2,0,1:T(4,128)(2,1)} %copy.52), calls=%async_computation | async-start | bytes 1048576 | tf_op jit(solution)/shard_map/all_to_all | solution.py:149
  42.9 12.5 %all-to-all-done = bf16[4,256,256]{2,0,1:T(4,128)(2,1)S(1)} async-done(((bf16[4,256,256]{2,0,1:T(4,128)(2,1)}), bf16[4,256,256]{2,0,1:T(4,128)(2,1)S(1)}, u32[]{:S(2)}, u32[]{:S(2)}) %all-to-all-start) | async-done | bytes 524320 | tf_op jit(solution)/shard_map/all_to_all | solution.py:149
  55.8 1.4 reshape.100
  57.5 1.4 reshape.99
  59.2 0.4 reshape.101
  59.6 2.6 %fusion.52 = f32[64,4,16,16]{3,2,1,0:T(8,128)} fusion(bf16[16,64,4,64]{3,2,1,0:T(4,128)(2,1)S(1)} %reshape.101, bf16[16,64,4,64]{3,2,1,0:T(4,128)(2,1)S(1)} %reshape_reshape.4), kind=kOutput, calls=%fused_computation.87 | convolution fusion | flops 8388608 | bytes 1310720 | tf_op jit(solution)/shard_map/tnhd,snhd->nhts/dot_general | solution.py:90
  62.3 4.9 %fusion.77 = (f32[64,4,16]{2,1,0:T(4,128)S(1)}, f32[64,4,16,16]{2,3,1,0:T(8,128)}) fusion(pred[16,16]{0,1:T(8,128)(4,1)S(1)} %iota_compare_fusion.7, bf16[16,64,4,64]{3,2,1,0:T(4,128)(2,1)} %reshape.99, bf16[16,64,4,64]{3,2,1,0:T(4,128)(2,1)} %reshape.100), kind=kOutput, calls=%fused_computation.119 | convolution fusion | flops 8650767 | bytes 1327360 | tf_op jit(solution)/shard_map/sub | solution.py:85
  67.2 5.8 %fusion.50 = bf16[16,64,4,64]{3,0,2,1:T(8,128)(2,1)} fusion(f32[64,4,16,16]{3,2,1,0:T(8,128)} %fusion.52, bf16[16,64,4,64]{3,2,1,0:T(4,128)(2,1)S(1)} %copy-done.4, f32[64,4,16,16]{2,3,1,0:T(8,128)} %get-tuple-element.187, f32[64,4,16]{2,1,0:T(4,128)S(1)} %get-tuple-element.186), kind=kOutput, calls=%fused_computation.78 | convolution fusion | flops 9113615 | bytes 1589248 | tf_op jit(solution)/shard_map/nhts,tnhd->snhd/dot_general | solution.py:96
  73.0 6.2 %fusion.48 = bf16[16,64,4,64]{3,0,2,1:T(8,128)(2,1)} fusion(f32[64,4,16,16]{3,2,1,0:T(8,128)} %fusion.52, bf16[16,64,4,64]{3,2,1,0:T(4,128)(2,1)} %reshape.99, f32[64,4,16,16]{2,3,1,0:T(8,128)} %get-tuple-element.187, f32[64,4,16]{2,1,0:T(4,128)S(1)} %get-tuple-element.186), kind=kOutput, calls=%fused_computation.76 | convolution fusion | flops 9113615 | bytes 1589248 | tf_op jit(solution)/shard_map/nhts,snhd->tnhd/dot_general | solution.py:95
  79.2 3.5 %fusion.49 = bf16[16,64,4,64]{3,0,2,1:T(8,128)(2,1)} fusion(bf16[16,64,4,64]{3,2,1,0:T(4,128)(2,1)S(1)} %reshape_reshape.4, f32[64,4,16,16]{2,3,1,0:T(8,128)} %get-tuple-element.187, f32[64,4,16]{2,1,0:T(4,128)} %copy-done.12), kind=kOutput, calls=%fused_computation.77 | convolution fusion | flops 8781824 | bytes 1327104 | tf_op jit(solution)/shard_map/nhts,tnhd->snhd/dot_general | solution.py:89
  82.7 1.7 copy.63
  84.5 0.7 reshape.103
  85.2 3.1 %copy.61 = bf16[16,64,4,64]{1,0,3,2:T(8,128)(2,1)S(1)} copy(bf16[16,64,4,64]{3,0,2,1:T(8,128)(2,1)} %fusion.48) | data formatting | bytes 1048576 | tf_op jit(solution)/shard_map/convert_element_type | solution.py:95
  88.3 0.7 reshape.102
  89.1 2.9 %copy.65 = bf16[16,64,4,64]{1,0,3,2:T(8,128)(2,1)S(1)} copy(bf16[16,64,4,64]{3,0,2,1:T(8,128)(2,1)} %fusion.49) | data formatting | bytes 1048576 | tf_op jit(solution)/shard_map/convert_element_type | solution.py:89
  92.0 0.7 reshape.104
  92.7 1.4 convolution_add_fusion.3
  94.5 1.2 fusion.51
  95.7 3.5 %all-to-all-start.1 = ((bf16[16,64,256]{2,1,0:T(8,128)(2,1)}), bf16[16,64,256]{2,1,0:T(8,128)(2,1)S(1)}, u32[]{:S(2)}, u32[]{:S(2)}) async-start(bf16[16,64,256]{2,1,0:T(8,128)(2,1)} %bitcast.30), calls=%async_computation.1 | async-start | bytes 1048576 | tf_op jit(solution)/shard_map/all_to_all | solution.py:152
  99.2 1.0 fusion.87
  100.2 1.0 fusion.86
  101.3 1.0 fusion.88
  102.3 9.8 %all-to-all-done.1 = bf16[16,64,256]{2,1,0:T(8,128)(2,1)S(1)} async-done(((bf16[16,64,256]{2,1,0:T(8,128)(2,1)}), bf16[16,64,256]{2,1,0:T(8,128)(2,1)S(1)}, u32[]{:S(2)}, u32[]{:S(2)}) %all-to-all-start.1) | async-done | bytes 524320 | tf_op jit(solution)/shard_map/all_to_all | solution.py:152
  112.4 15.7 %while.35 = (s32[]{:T(128)}, f32[4,256,256]{2,1,0:T(8,128)S(1)}, f32[4,256,256]{2,1,0:T(8,128)S(1)}, bf16[4,128,256]{2,1,0:T(8,128)(2,1)S(1)}, bf16[4,256,256]{2...) while((s32[]{:T(128)}, f32[4,256,256]{2,1,0:T(8,128)S(1)}, ...), condition=%wide.region_7.8_spmd.clone, body=%wide.region_6.7_spmd.sunk.clone | while | flops 370671616 | bytes 3479153 | solution.py:157
  112.4 1.2 convolution_multiply_fusion.3
  113.6 1.3 fusion.149
  115.0 1.3 fusion.148
  116.3 1.2 convolution_multiply_fusion.3
  117.6 1.3 fusion.149
  118.9 1.3 fusion.148
  120.3 1.2 convolution_multiply_fusion.3
  121.5 1.3 fusion.149
  122.9 1.3 fusion.148
  124.2 1.2 convolution_multiply_fusion.3
  125.4 1.3 fusion.149
  126.8 1.3 fusion.148
  128.1 0.8 reduce_sum.38
  129.0 56.0 %all-reduce.5.cloned.1.call-done = (f32[256,256]{1,0:T(8,128)}, f32[256,256]{1,0:T(8,128)}, f32[256,256]{1,0:T(8,128)}, f32[256,256]{1,0:T(8,128)}) async-done(((f32[256,256]{1,0:T(8,128)}, f32[256,256]{1,0:T(8,128)}, f32[256,256]{1,0:T(8,128)}, f32[256,256]{1,0:T(8,128)}), (f32[256,256]{1,0:T(8,128)}, f32[256,256]{1,0:T(8,128)}, f32[256,256]{1,0:T(8,128)}, ...) | async-done | bytes 1048592 | tf_op jit(solution)/shard_map/psum | solution.py:169
  185.1 3.9 %collective-permute-done.1 = bf16[4,128,256]{2,1,0:T(8,128)(2,1)S(1)} collective-permute-done((bf16[4,128,256]{2,1,0:T(8,128)(2,1)S(1)}, bf16[4,128,256]{2,1,0:T(8,128)(2,1)S(1)}, u32[]{:S(2)}, u32[]{:S(2)}) %collective-permute-start.1) | collective-permute-done | bytes 262176 | tf_op jit(solution)/shard_map/ppermute | solution.py:12
  189.0 1.5 convolution_add_fusion.4
  190.5 49.2 %all-reduce.7.cloned.1.call-done = (f32[256,256]{1,0:T(8,128)}, f32[256,256]{1,0:T(8,128)}, f32[256,256]{1,0:T(8,128)}, f32[256,256]{1,0:T(8,128)}) async-done(((f32[256,256]{1,0:T(8,128)}, f32[256,256]{1,0:T(8,128)}, f32[256,256]{1,0:T(8,128)}, f32[256,256]{1,0:T(8,128)}), (f32[256,256]{1,0:T(8,128)}, f32[256,256]{1,0:T(8,128)}, f32[256,256]{1,0:T(8,128)}, ...) | async-done | bytes 1048592 | tf_op jit(solution)/shard_map/psum | solution.py:168
  239.7 1.7 copy.141
  241.3 1.7 copy.142
  243.0 1.7 copy.143
  244.7 1.7 copy.144
  (89 shorter events, 5.1 us)
Async XLA Ops:
  7.2 48.3 %copy-start = (bf16[256,256]{1,0:T(8,128)(2,1)S(1)}, bf16[256,256]{1,0:T(8,128)(2,1)}, u32[]{:S(2)}) copy-start(bf16[256,256]{1,0:T(8,128)(2,1)} %param.20) | copy-start | bytes 393220
  8.7 14.8 %copy-start.1 = (bf16[4,256,256]{2,1,0:T(8,128)(2,1)S(1)}, bf16[4,256,256]{2,1,0:T(8,128)(2,1)}, u32[]{:S(2)}) copy-start(bf16[4,256,256]{2,1,0:T(8,128)(2,1)} %param.14) | copy-start | bytes 1572868
  8.7 14.8 %copy-start.2 = (bf16[256,256]{1,0:T(8,128)(2,1)S(1)}, bf16[256,256]{1,0:T(8,128)(2,1)}, u32[]{:S(2)}) copy-start(bf16[256,256]{1,0:T(8,128)(2,1)} %param.19) | copy-start | bytes 393220
  15.9 7.4 %collective-permute-start = (bf16[4,128,256]{2,1,0:T(8,128)(2,1)S(1)}, bf16[4,128,256]{2,1,0:T(8,128)(2,1)S(1)}, u32[]{:S(2)}, u32[]{:S(2)}) collective-permute-start(bf16[4,128,256]{2,1,0:T(8,128)(2,1)S(1)} %select_select_fusion), channel_id=1, source_target_pairs={{0,1},{1,2},{2,3},{3,4},{4,5},{5,6},{6,7},{7,0},{8,9},{9,10},{10,1... | collective-permute-start | bytes 786440 | tf_op jit(solution)/shard_map/ppermute | solution.py:12
  35.6 1.2 copy-start.5
  35.6 19.8 %copy-start.11 = (bf16[4,256,256]{2,1,0:T(8,128)(2,1)}, bf16[4,256,256]{2,1,0:T(8,128)(2,1)S(1)}, u32[]{:S(2)}) copy-start(bf16[4,256,256]{2,1,0:T(8,128)(2,1)S(1)} %get-tuple-element.426) | copy-start | bytes 1572868
  35.6 6.8 %copy-start.3 = (bf16[16,1,1,64,256]{4,3,2,1,0:T(8,128)(2,1)S(1)}, bf16[16,1,1,64,256]{4,3,2,1,0:T(8,128)(2,1)}, u32[]{:S(2)}) copy-start(bf16[16,1,1,64,256]{4,3,2,1,0:T(8,128)(2,1)} %param.23) | copy-start | bytes 1572868
  36.8 18.5 %all-to-all-start = ((bf16[4,256,256]{2,0,1:T(4,128)(2,1)}), bf16[4,256,256]{2,0,1:T(4,128)(2,1)S(1)}, u32[]{:S(2)}, u32[]{:S(2)}) async-start(bf16[4,256,256]{2,0,1:T(4,128)(2,1)} %copy.52), calls=%async_computation | async-start | bytes 1048576 | tf_op jit(solution)/shard_map/all_to_all | solution.py:149
  55.4 1.8 copy-start.8
  55.8 3.1 %copy-start.7 = (bf16[256,256]{1,0:T(8,128)(2,1)S(1)}, bf16[256,256]{1,0:T(8,128)(2,1)}, u32[]{:S(2)}) copy-start(bf16[256,256]{1,0:T(8,128)(2,1)} %param.22) | copy-start | bytes 393220
  62.2 4.9 %copy-start.4 = (bf16[16,64,4,64]{3,2,1,0:T(4,128)(2,1)S(1)}, bf16[16,64,4,64]{3,2,1,0:T(4,128)(2,1)}, u32[]{:S(2)}) copy-start(bf16[16,64,4,64]{3,2,1,0:T(4,128)(2,1)} %reshape.100) | copy-start | bytes 1572868
  67.2 5.8 %copy-start.12 = (f32[64,4,16]{2,1,0:T(4,128)}, f32[64,4,16]{2,1,0:T(4,128)S(1)}, u32[]{:S(2)}) copy-start(f32[64,4,16]{2,1,0:T(4,128)S(1)} %get-tuple-element.186) | copy-start | bytes 49156
  79.2 3.5 %copy-start.6 = (bf16[16,64,4,64]{3,0,2,1:T(8,128)(2,1)S(1)}, bf16[16,64,4,64]{3,0,2,1:T(8,128)(2,1)}, u32[]{:S(2)}) copy-start(bf16[16,64,4,64]{3,0,2,1:T(8,128)(2,1)} %fusion.50) | copy-start | bytes 1572868
  92.7 1.5 copy-start.9
  95.7 16.5 %all-to-all-start.1 = ((bf16[16,64,256]{2,1,0:T(8,128)(2,1)}), bf16[16,64,256]{2,1,0:T(8,128)(2,1)S(1)}, u32[]{:S(2)}, u32[]{:S(2)}) async-start(bf16[16,64,256]{2,1,0:T(8,128)(2,1)} %bitcast.30), calls=%async_computation.1 | async-start | bytes 1048576 | tf_op jit(solution)/shard_map/all_to_all | solution.py:152
  99.1 85.9 %all-reduce.5.cloned.1.call-start = ((), (), s32[]{:S(2)}) async-start(), calls=%async_computation.2 | async-start | bytes 2097152 | tf_op jit(solution)/shard_map/psum | solution.py:169
  128.1 60.9 %copy-start.10 = (s32[4,128]{1,0:T(4,128)S(1)}, s32[4,128]{1,0:T(4,128)}, u32[]{:S(2)}) copy-start(s32[4,128]{1,0:T(4,128)} %param.17) | copy-start | bytes 6148
  128.9 110.7 %all-reduce.7.cloned.1.call-start = ((), (), s32[]{:S(2)}) async-start(), calls=%async_computation.3 | async-start | bytes 2097152 | tf_op jit(solution)/shard_map/psum | solution.py:168
  185.0 3.9 %collective-permute-start.1 = (bf16[4,128,256]{2,1,0:T(8,128)(2,1)S(1)}, bf16[4,128,256]{2,1,0:T(8,128)(2,1)S(1)}, u32[]{:S(2)}, u32[]{:S(2)}) collective-permute-start(bf16[4,128,256]{2,1,0:T(8,128)(2,1)S(1)} %get-tuple-element.126), channel_id=1, source_target_pairs={{0,7},{1,0},{2,1},{3,2},{4,3},{5,4},{6,5},{7,6},{8,15},{9,8},{10,9... | collective-permute-start | bytes 786440 | tf_op jit(solution)/shard_map/ppermute | solution.py:12
Sparse Core Ops, SparseCore 0:
  129.0 55.9 all-reduce.4
  187.6 52.0 all-reduce.6
